TPU v7x, 512 devices: a whole 4x8x8 slice. The times are simulated.
512 devices in a mesh: seq: 64 (over x, z_lo, y), tp: 8 (over z_hi, core).
Axes of the slice: x: 4, y: 8, z: 8 (z_hi: 4, z_lo: 2; z = z_hi * 2 + z_lo), core: 2. Of those that a mesh axis runs over, the one named last changes fastest.
Arguments:
- tokens: bfloat16 [16384, 2048], P('seq', 'tp'), may hold values from -6 to 6
- key_weight: bfloat16 [2048, 2048], P(None, 'tp'), may hold values from -0.125 to 0.125
- value_weight: bfloat16 [2048, 2048], P(None, 'tp'), may hold values from -0.125 to 0.125
- queries: bfloat16 [16384, 2, 2048], P('seq', None, 'tp'), may hold values from -256 to 256
- prompt_pages: int32 [16], replicated, may hold values from 1 to 97, 1024 in all
- page_table: int32 [1024], P('seq'), may hold values from 0 to 1023, as said below
Outputs:
- attended: bfloat16 [16384, 2, 2048], P('seq', None, 'tp')
- cache: bfloat16 [1024, 16, 2, 2048], P('seq', None, None, 'tp')
Inputs may be any that keep to these rules, and one draw needn't show every extreme that they name: `prompt_pages`: lengths of the prompts in pages; they sum to 1024 and the longest has exactly 97 pages. `page_table`: A permutation of the cache pages. Page c is held by owner c // 16 of seq. At most 1 pages of one stream block go to one owner, some block sends exactly 1 to one owner, and every owner receives 256/16 pages.
All inputs are finite; a program needn't handle non-finite values.
Results may differ from a plain program's by a relative error of at most 0.03.
Values may be sent and summed in bfloat16 or wider, within the bound.
No kernel may reach another device: no remote copies, remote signals or barrier semaphores. Data moves between devices by JAX's collectives and lax.ppermute only.
A program may use at most 64 MiB of HBM per device.

v0:
```python
import math

import jax
import jax.numpy as jnp
from jax import lax
from jax.sharding import PartitionSpec as P


HD = 128
TOPK = 2
PAGE = 16
BACK = 6


def from_behind(value, axis, by):
    peers = lax.axis_size(axis)
    pairs = [(i, i + by) for i in range(peers) if 0 <= i + by < peers]
    return lax.ppermute(value, axis, pairs)


def segment_info(positions, prompt_pages):
    ends = PAGE * jnp.cumsum(prompt_pages)
    below = ends[None, :] <= positions[:, None]
    segment = jnp.sum(below.astype(jnp.int32), axis=1)
    start = jnp.max(jnp.where(below, ends[None, :], 0), axis=1)
    return (segment, positions - start)


def rotate_heads(raw, offsets):
    half = HD // 2
    inverse = 10000.0 ** (-(2.0 * jnp.arange(half, dtype=jnp.float32)) / HD)
    angle = offsets.astype(jnp.float32)[:, None] * inverse[None, :]
    cosine = jnp.cos(angle)[:, None, :]
    sine = jnp.sin(angle)[:, None, :]
    lower = raw[..., :half]
    upper = raw[..., half:]
    return jnp.concatenate([lower * cosine - upper * sine, upper * cosine + lower * sine], axis=-1)


def body(tokens, key_weight, value_weight, queries, prompt_pages, page_table):
    block_rows = tokens.shape[0]
    width = key_weight.shape[1]
    local_heads = width // HD
    devices = lax.axis_size("seq")
    first_row = lax.axis_index("seq") * block_rows
    positions = first_row + jnp.arange(block_rows, dtype=jnp.int32)
    segment, offsets = segment_info(positions, prompt_pages)
    piece = lax.all_gather(tokens, "tp", axis=1, tiled=True)
    raw_keys = jnp.dot(piece, key_weight, preferred_element_type=jnp.float32)
    raw_values = jnp.dot(piece, value_weight, preferred_element_type=jnp.float32)
    keys = rotate_heads(raw_keys.reshape(block_rows, local_heads, HD), offsets).astype(jnp.bfloat16)
    values = raw_values.astype(jnp.bfloat16)
    key_value = jnp.stack([keys.reshape(block_rows, width), values], axis=1)
    blocks = [key_value]
    for distance in range(1, BACK + 1):
        blocks.append(from_behind(key_value, "seq", distance))
    query = queries.reshape(block_rows, TOPK, local_heads, HD)
    scale = 1.0 / math.sqrt(HD)
    masks = []
    for distance in range(BACK + 1):
        key_place = positions - distance * block_rows
        key_segment, _ = segment_info(key_place, prompt_pages)
        allowed = (segment[:, None] == key_segment[None, :]) & (
            key_place[None, :] <= positions[:, None]
        )
        masks.append(allowed & (key_place[None, :] >= 0))

    def block_scores(expert_query, block, allowed):
        key_heads = block[:, 0].reshape(block_rows, local_heads, HD)
        scores = (
            jnp.einsum("qhd,khd->qhk", expert_query, key_heads, preferred_element_type=jnp.float32)
            * scale
        )
        return jnp.where(allowed[:, None, :], scores, -jnp.inf)

    outputs = []
    for expert in range(TOPK):
        expert_query = query[:, expert]
        score_list = []
        for distance in range(BACK + 1):
            block = blocks[distance]
            allowed = masks[distance]

            def compute(block=block, allowed=allowed):
                return block_scores(expert_query, block, allowed)

            score_list.append(compute())
        peak = jnp.max(score_list[0], axis=-1)
        for distance in range(1, BACK + 1):
            peak = jnp.maximum(peak, jnp.max(score_list[distance], axis=-1))
        total = jnp.zeros((block_rows, local_heads), jnp.float32)
        summed = jnp.zeros((block_rows, local_heads, HD), jnp.float32)
        for distance in range(BACK + 1):
            block = blocks[distance]
            allowed = masks[distance]
            scores = score_list[distance]

            def accumulate(state, block=block, scores=scores):
                weight = jnp.exp(scores - peak[..., None])
                rounded = weight.astype(jnp.bfloat16)
                value_heads = block[:, 1].reshape(block_rows, local_heads, HD)
                product = jnp.einsum(
                    "qhk,khd->qhd", rounded, value_heads, preferred_element_type=jnp.float32
                )
                return (state[0] + jnp.sum(weight, axis=-1), state[1] + product)

            total, summed = accumulate((total, summed))
        outputs.append((summed / total[..., None]).astype(jnp.bfloat16))
    attended = jnp.stack(outputs, axis=1).reshape(block_rows, TOPK, width)
    pages_dev = block_rows // PAGE
    capacity = max(1, pages_dev // devices)
    owner = page_table // pages_dev
    place_on_owner = page_table % pages_dev
    page_order = jnp.arange(pages_dev, dtype=jnp.int32)
    earlier = (owner[:, None] == owner[None, :]) & (page_order[None, :] < page_order[:, None])
    rank = jnp.sum(earlier.astype(jnp.int32), axis=1)
    target = (owner[None, None, :] == jnp.arange(devices, dtype=jnp.int32)[:, None, None]) & (
        rank[None, None, :] == jnp.arange(capacity, dtype=jnp.int32)[None, :, None]
    )
    pages = key_value.reshape(pages_dev, PAGE, 2, width)
    page_index = jnp.sum(jnp.where(target, page_order[None, None, :], 0), axis=2)
    outgoing = pages[page_index.reshape(-1)]
    labels = jnp.sum(jnp.where(target, place_on_owner[None, None, :] + 1, 0), axis=2) - 1
    incoming = lax.all_to_all(outgoing, "seq", split_axis=0, concat_axis=0, tiled=True)
    arrived = lax.all_to_all(labels, "seq", split_axis=0, concat_axis=0, tiled=True)
    slots = jnp.arange(devices * capacity, dtype=jnp.int32)
    source_slot = jnp.sum(
        jnp.where(arrived.reshape(-1)[None, :] == page_order[:, None], slots[None, :], 0), axis=1
    )
    cache = incoming[source_slot]
    return (attended, cache)


def solution(mesh):
    in_specs = (P("seq", "tp"), P(None, "tp"), P(None, "tp"), P("seq", None, "tp"), P(), P("seq"))
    out_specs = (P("seq", None, "tp"), P("seq", None, None, "tp"))
    return jax.shard_map(body, mesh=mesh, in_specs=in_specs, out_specs=out_specs, check_vma=False)
```

profile of v0, /device:TPU:94, one launch (start us, length us, event | category | flops | bytes accessed | tf_op | source)
XLA Modules:
  0.0 186.9 jit_solution(4498426820051926726)
XLA Ops:
  9.0 11.4 %all-to-all-start.1 = ((s32[64,1,1]{2,1,0:T(1,128)}), s32[64,1,1]{2,1,0:T(1,128)S(1)}, u32[]{:S(2)}, u32[]{:S(2)}) async-start(s32[64,1,1]{2,1,0:T(1,128)} %copy.259), calls=%async_computation.1 | async-start | bytes 65536 | tf_op jit(solution)/shard_map/all_to_all | solution.py:125
  22.3 1.2 multiply_cosine_fusion
  23.5 2.0 %and_and_fusion.5 = (pred[256,256]{0,1:T(8,128)(4,1)}, pred[256,256]{0,1:T(8,128)(4,1)}, pred[256,256]{0,1:T(8,128)(4,1)}, pred[256,256]{0,1:T(8,128)(4,1)}, pre...) fusion(s32[256]{0:T(256)S(1)} %get-tuple-element.90, s32[256]{0:T(256)S(1)} %get-tuple-element.35, s32[256]{0:T(256)S(1)} %fusion.129, ...), kind=kLoop, calls=%fused_computation.140 | loop fusion | flops 1572864 | bytes 407040 | tf_op jit(solution)/shard_map/and | solution.py:66
  25.5 0.9 copy.212
  26.4 1.2 reduce.3
  27.8 18.3 %all-gather.2.cloned.1.call-done = bf16[256,2048]{1,0:T(8,128)(2,1)} async-done(((bf16[256,256]{1,0:T(8,128)(2,1)}), bf16[256,2048]{1,0:T(8,128)(2,1)}) %all-gather.2.cloned.1.call-update) | async-done | bytes 1048592 | tf_op jit(solution)/shard_map/all_gather | solution.py:48
  46.1 1.7 fusion.155
  48.1 0.8 copy.283
  48.9 1.1 multiply_subtract_fusion
  52.7 1.3 collective-permute-start.5
  54.0 1.3 collective-permute-start.4
  55.3 4.7 %collective-permute-start.3 = (bf16[256,2,256]{2,0,1:T(8,128)(2,1)}, bf16[256,2,256]{2,0,1:T(8,128)(2,1)S(1)}, u32[]{:S(2)}, u32[]{:S(2)}) collective-permute-start(bf16[256,2,256]{2,0,1:T(8,128)(2,1)} %pad_maximum_fusion), channel_id=1, source_target_pairs={{0,32},{8,40},{16,48},{24,56},{32,64},{40,72},{48,80},{56,88},{64,... | collective-permute-start | bytes 786440 | tf_op jit(solution)/shard_map/ppermute | solution.py:18
  59.9 1.9 %collective-permute-start.2 = (bf16[256,2,256]{2,0,1:T(8,128)(2,1)}, bf16[256,2,256]{2,0,1:T(8,128)(2,1)S(1)}, u32[]{:S(2)}, u32[]{:S(2)}) collective-permute-start(bf16[256,2,256]{2,0,1:T(8,128)(2,1)} %pad_maximum_fusion), channel_id=1, source_target_pairs={{0,24},{8,32},{16,40},{24,48},{32,56},{40,64},{48,72},{56,80},{64,... | collective-permute-start | bytes 786440 | tf_op jit(solution)/shard_map/ppermute | solution.py:18
  61.9 1.9 %collective-permute-start = (bf16[256,2,256]{2,0,1:T(8,128)(2,1)}, bf16[256,2,256]{2,0,1:T(8,128)(2,1)}, u32[]{:S(2)}, u32[]{:S(2)}) collective-permute-start(bf16[256,2,256]{2,0,1:T(8,128)(2,1)} %pad_maximum_fusion), channel_id=1, source_target_pairs={{0,8},{8,16},{16,24},{24,32},{32,40},{40,48},{48,56},{56,64},{64,7... | collective-permute-start | bytes 786440 | tf_op jit(solution)/shard_map/ppermute | solution.py:18
  63.9 1.7 gather_fusion
  65.6 22.4 %all-to-all-start = ((bf16[64,16,2,256]{3,1,2,0:T(8,128)(2,1)}), bf16[64,16,2,256]{3,1,2,0:T(8,128)(2,1)}, u32[]{:S(2)}, u32[]{:S(2)}) async-start(bf16[64,16,2,256]{3,1,2,0:T(8,128)(2,1)} %gather_fusion), calls=%async_computation | async-start | bytes 2097152 | tf_op jit(solution)/shard_map/all_to_all | solution.py:124
  88.1 1.6 fusion.153
  90.0 5.6 %collective-permute-done.4 = bf16[256,2,256]{2,0,1:T(8,128)(2,1)S(1)} collective-permute-done((bf16[256,2,256]{2,0,1:T(8,128)(2,1)}, bf16[256,2,256]{2,0,1:T(8,128)(2,1)S(1)}, u32[]{:S(2)}, u32[]{:S(2)}) %collective-permute-start.4) | collective-permute-done | bytes 262176 | tf_op jit(solution)/shard_map/ppermute | solution.py:18
  95.6 22.4 %collective-permute-start.1 = (bf16[256,2,256]{2,0,1:T(8,128)(2,1)}, bf16[256,2,256]{2,0,1:T(8,128)(2,1)}, u32[]{:S(2)}, u32[]{:S(2)}) collective-permute-start(bf16[256,2,256]{2,0,1:T(8,128)(2,1)} %pad_maximum_fusion), channel_id=1, source_target_pairs={{0,16},{8,24},{16,32},{24,40},{32,48},{40,56},{48,64},{56,72},{64,... | collective-permute-start | bytes 786440 | tf_op jit(solution)/shard_map/ppermute | solution.py:18
  118.9 1.6 fusion.149
  122.3 1.6 fusion.150
  123.9 1.1 fusion.143
  126.5 1.6 fusion.151
  128.1 1.7 fusion.144
  129.8 1.6 fusion.135
  132.2 2.6 %fusion.154 = (f32[256,2]{0,1:T(2,128)}, f32[256,2,256]{0,2,1:T(8,128)}) fusion(bf16[256,2,2,128]{0,3,2,1:T(8,128)(2,1)} %bitcast.203, bf16[256,2,128]{2,1,0:T(2,128)(2,1)} %reshape_squeeze.48, pred[256,256]{0,1:T(8,128)(4,1)} %get-tuple-element.52), kind=kOutput, calls=%fused_computation.232 | convolution fusion | flops 33947136 | bytes 854016 | tf_op jit(solution)/shard_map/qhd,khd->qhk/dot_general | solution.py:71
  134.8 1.6 fusion.147
  136.4 1.6 fusion.139
  138.8 2.6 %fusion.148 = (f32[256,2]{0,1:T(2,128)}, f32[256,2,256]{0,2,1:T(8,128)}) fusion(bf16[256,2,2,128]{0,3,2,1:T(8,128)(2,1)} %bitcast.204, bf16[256,2,128]{2,1,0:T(2,128)(2,1)} %reshape_squeeze.53, pred[256,256]{0,1:T(8,128)(4,1)} %get-tuple-element.55), kind=kOutput, calls=%fused_computation.226 | convolution fusion | flops 33947136 | bytes 854016 | tf_op jit(solution)/shard_map/qhd,khd->qhk/dot_general | solution.py:71
  141.4 1.6 fusion.141
  143.0 1.6 fusion.134
  145.4 2.6 %fusion.152 = (f32[256,2]{0,1:T(2,128)}, f32[256,2,256]{0,2,1:T(8,128)}) fusion(bf16[256,2,2,128]{0,3,2,1:T(8,128)(2,1)} %bitcast.205, bf16[256,2,128]{2,1,0:T(2,128)(2,1)} %reshape_squeeze.49, pred[256,256]{0,1:T(8,128)(4,1)} %and_and_fusion.4), kind=kOutput, calls=%fused_computation.230 | convolution fusion | flops 33947136 | bytes 854016 | tf_op jit(solution)/shard_map/qhd,khd->qhk/dot_general | solution.py:71
  148.0 1.6 fusion.145
  149.6 1.0 copy.276
  150.6 1.7 copy.278
  152.3 1.7 copy.279
  154.7 1.7 copy.281
  156.4 1.0 copy.277
  158.2 1.3 fusion.92
  163.0 0.9 fusion.40
  163.9 1.8 copy.256
  167.1 1.9 %fusion.58 = (f32[256,2]{0,1:T(2,128)S(1)}, f32[256,2]{0,1:T(2,128)S(1)}, f32[256,2]{0,1:T(2,128)S(1)}, f32[256,2]{0,1:T(2,128)S(1)}, f32[256,2]{0,1:T(2,128)S(1...) fusion(f32[256,2,256]{0,2,1:T(8,128)} %get-tuple-element.75, f32[256,2]{0,1:T(2,128)S(1)} %maximum_maximum_fusion, ...), kind=kLoop, calls=%fused_computation.93 | loop fusion | flops 1831424 | bytes 3686400 | tf_op jit(solution)/shard_map/reduce_sum | solution.py:105
  171.9 0.8 copy-done.4
  173.0 0.8 copy-done.8
  174.0 0.8 copy-done.10
  176.1 1.3 pad_maximum_fusion.1
  177.4 1.8 gather_fusion.1
  179.2 0.9 copy.260
  (166 shorter events, 24.1 us)
Async XLA Ops:
  7.2 39.0 %copy-start = (bf16[2048,256]{1,0:T(8,128)(2,1)S(1)}, bf16[2048,256]{1,0:T(8,128)(2,1)}, u32[]{:S(2)}) copy-start(bf16[2048,256]{1,0:T(8,128)(2,1)} %param.7) | copy-start | bytes 3145732
  7.2 38.9 %all-gather.2.cloned.1.call-start = ((), (), s32[]{:S(2)}) async-start(), calls=%async_computation.2 | async-start | bytes 1179648 | tf_op jit(solution)/shard_map/all_gather | solution.py:48
  9.0 17.5 %all-to-all-start.1 = ((s32[64,1,1]{2,1,0:T(1,128)}), s32[64,1,1]{2,1,0:T(1,128)S(1)}, u32[]{:S(2)}, u32[]{:S(2)}) async-start(s32[64,1,1]{2,1,0:T(1,128)} %copy.259), calls=%async_computation.1 | async-start | bytes 65536 | tf_op jit(solution)/shard_map/all_to_all | solution.py:125
  23.5 2.0 %copy-start.23 = (bf16[256,2,256]{2,1,0:T(2,128)(2,1)S(1)}, bf16[256,2,256]{2,1,0:T(2,128)(2,1)}, u32[]{:S(2)}) copy-start(bf16[256,2,256]{2,1,0:T(2,128)(2,1)} %param.9) | copy-start | bytes 786436
  48.0 3.0 %copy-start.21 = (bf16[2048,256]{1,0:T(8,128)(2,1)S(1)}, bf16[2048,256]{1,0:T(8,128)(2,1)}, u32[]{:S(2)}) copy-start(bf16[2048,256]{1,0:T(8,128)(2,1)} %param.8) | copy-start | bytes 3145732
  48.9 2.2 %copy-start.1 = (bf16[256,2048]{1,0:T(8,128)(2,1)S(1)}, bf16[256,2048]{1,0:T(8,128)(2,1)}, u32[]{:S(2)}) copy-start(bf16[256,2048]{1,0:T(8,128)(2,1)} %all-gather.2.cloned.1.call-done) | copy-start | bytes 3145732
  51.1 0.9 copy-start.22
  52.7 83.8 %collective-permute-start.5 = (bf16[256,2,256]{2,0,1:T(8,128)(2,1)}, bf16[256,2,256]{2,0,1:T(8,128)(2,1)}, u32[]{:S(2)}, u32[]{:S(2)}) collective-permute-start(bf16[256,2,256]{2,0,1:T(8,128)(2,1)} %pad_maximum_fusion), channel_id=1, source_target_pairs={{0,48},{8,56},{16,64},{24,72},{32,80},{40,88},{48,96},{56,104},{64... | collective-permute-start | bytes 786440 | tf_op jit(solution)/shard_map/ppermute | solution.py:18
  54.0 41.6 %collective-permute-start.4 = (bf16[256,2,256]{2,0,1:T(8,128)(2,1)}, bf16[256,2,256]{2,0,1:T(8,128)(2,1)S(1)}, u32[]{:S(2)}, u32[]{:S(2)}) collective-permute-start(bf16[256,2,256]{2,0,1:T(8,128)(2,1)} %pad_maximum_fusion), channel_id=1, source_target_pairs={{0,40},{8,48},{16,56},{24,64},{32,72},{40,80},{48,88},{56,96},{64,... | collective-permute-start | bytes 786440 | tf_op jit(solution)/shard_map/ppermute | solution.py:18
  55.3 65.5 %collective-permute-start.3 = (bf16[256,2,256]{2,0,1:T(8,128)(2,1)}, bf16[256,2,256]{2,0,1:T(8,128)(2,1)S(1)}, u32[]{:S(2)}, u32[]{:S(2)}) collective-permute-start(bf16[256,2,256]{2,0,1:T(8,128)(2,1)} %pad_maximum_fusion), channel_id=1, source_target_pairs={{0,32},{8,40},{16,48},{24,56},{32,64},{40,72},{48,80},{56,88},{64,... | collective-permute-start | bytes 786440 | tf_op jit(solution)/shard_map/ppermute | solution.py:18
  59.9 65.0 %collective-permute-start.2 = (bf16[256,2,256]{2,0,1:T(8,128)(2,1)}, bf16[256,2,256]{2,0,1:T(8,128)(2,1)S(1)}, u32[]{:S(2)}, u32[]{:S(2)}) collective-permute-start(bf16[256,2,256]{2,0,1:T(8,128)(2,1)} %pad_maximum_fusion), channel_id=1, source_target_pairs={{0,24},{8,32},{16,40},{24,48},{32,56},{40,64},{48,72},{56,80},{64,... | collective-permute-start | bytes 786440 | tf_op jit(solution)/shard_map/ppermute | solution.py:18
  61.9 67.9 %collective-permute-start = (bf16[256,2,256]{2,0,1:T(8,128)(2,1)}, bf16[256,2,256]{2,0,1:T(8,128)(2,1)}, u32[]{:S(2)}, u32[]{:S(2)}) collective-permute-start(bf16[256,2,256]{2,0,1:T(8,128)(2,1)} %pad_maximum_fusion), channel_id=1, source_target_pairs={{0,8},{8,16},{16,24},{24,32},{32,40},{40,48},{48,56},{56,64},{64,7... | collective-permute-start | bytes 786440 | tf_op jit(solution)/shard_map/ppermute | solution.py:18
  65.6 22.4 %copy-start.24 = (bf16[256,2,256]{0,2,1:T(8,128)(2,1)S(1)}, bf16[256,2,256]{0,2,1:T(8,128)(2,1)}, u32[]{:S(2)}) copy-start(bf16[256,2,256]{0,2,1:T(8,128)(2,1)} %copy.212) | copy-start | bytes 786436
  65.6 22.4 %copy-start.41 = (pred[256,256]{0,1:T(8,128)(4,1)S(1)}, pred[256,256]{0,1:T(8,128)(4,1)}, u32[]{:S(2)}) copy-start(pred[256,256]{0,1:T(8,128)(4,1)} %get-tuple-element.57) | copy-start | bytes 196612
  65.6 111.8 %all-to-all-start = ((bf16[64,16,2,256]{3,1,2,0:T(8,128)(2,1)}), bf16[64,16,2,256]{3,1,2,0:T(8,128)(2,1)}, u32[]{:S(2)}, u32[]{:S(2)}) async-start(bf16[64,16,2,256]{3,1,2,0:T(8,128)(2,1)} %gather_fusion), calls=%async_computation | async-start | bytes 2097152 | tf_op jit(solution)/shard_map/all_to_all | solution.py:124
  95.6 47.4 %collective-permute-start.1 = (bf16[256,2,256]{2,0,1:T(8,128)(2,1)}, bf16[256,2,256]{2,0,1:T(8,128)(2,1)}, u32[]{:S(2)}, u32[]{:S(2)}) collective-permute-start(bf16[256,2,256]{2,0,1:T(8,128)(2,1)} %pad_maximum_fusion), channel_id=1, source_target_pairs={{0,16},{8,24},{16,32},{24,40},{32,48},{40,56},{48,64},{56,72},{64,... | collective-permute-start | bytes 786440 | tf_op jit(solution)/shard_map/ppermute | solution.py:18
  118.1 0.8 copy-start.40
  122.3 1.6 copy-start.39
  126.5 1.6 copy-start.25
  126.5 1.6 copy-start.37
  132.1 2.7 %copy-start.26 = (bf16[256,2,256]{0,2,1:T(8,128)(2,1)S(1)}, bf16[256,2,256]{0,2,1:T(8,128)(2,1)}, u32[]{:S(2)}) copy-start(bf16[256,2,256]{0,2,1:T(8,128)(2,1)} %copy.212) | copy-start | bytes 786436
  132.1 2.7 %copy-start.33 = (bf16[256,2,128]{2,1,0:T(2,128)(2,1)S(1)}, bf16[256,2,128]{2,1,0:T(2,128)(2,1)}, u32[]{:S(2)}) copy-start(bf16[256,2,128]{2,1,0:T(2,128)(2,1)} %reshape_squeeze.48) | copy-start | bytes 393220
  132.1 2.7 %copy-start.35 = (pred[256,256]{0,1:T(8,128)(4,1)S(1)}, pred[256,256]{0,1:T(8,128)(4,1)}, u32[]{:S(2)}) copy-start(pred[256,256]{0,1:T(8,128)(4,1)} %get-tuple-element.52) | copy-start | bytes 196612
  138.8 2.6 %copy-start.27 = (bf16[256,2,256]{0,2,1:T(8,128)(2,1)S(1)}, bf16[256,2,256]{0,2,1:T(8,128)(2,1)}, u32[]{:S(2)}) copy-start(bf16[256,2,256]{0,2,1:T(8,128)(2,1)} %copy.212) | copy-start | bytes 786436
  138.8 2.6 %copy-start.29 = (bf16[256,2,128]{2,1,0:T(2,128)(2,1)S(1)}, bf16[256,2,128]{2,1,0:T(2,128)(2,1)}, u32[]{:S(2)}) copy-start(bf16[256,2,128]{2,1,0:T(2,128)(2,1)} %reshape_squeeze.53) | copy-start | bytes 393220
  138.8 2.6 %copy-start.34 = (pred[256,256]{0,1:T(8,128)(4,1)S(1)}, pred[256,256]{0,1:T(8,128)(4,1)}, u32[]{:S(2)}) copy-start(pred[256,256]{0,1:T(8,128)(4,1)} %get-tuple-element.55) | copy-start | bytes 196612
  145.4 2.7 %copy-start.28 = (bf16[256,2,256]{0,2,1:T(8,128)(2,1)S(1)}, bf16[256,2,256]{0,2,1:T(8,128)(2,1)}, u32[]{:S(2)}) copy-start(bf16[256,2,256]{0,2,1:T(8,128)(2,1)} %copy.212) | copy-start | bytes 786436
  145.4 2.7 %copy-start.30 = (bf16[256,2,128]{2,1,0:T(2,128)(2,1)S(1)}, bf16[256,2,128]{2,1,0:T(2,128)(2,1)}, u32[]{:S(2)}) copy-start(bf16[256,2,128]{2,1,0:T(2,128)(2,1)} %reshape_squeeze.49) | copy-start | bytes 393220
  145.4 2.7 %copy-start.42 = (pred[256,256]{0,1:T(8,128)(4,1)S(1)}, pred[256,256]{0,1:T(8,128)(4,1)}, u32[]{:S(2)}) copy-start(pred[256,256]{0,1:T(8,128)(4,1)} %and_and_fusion.4) | copy-start | bytes 196612
  157.4 2.1 %copy-start.6 = (f32[256,2,256]{0,2,1:T(8,128)S(1)}, f32[256,2,256]{0,2,1:T(8,128)}, u32[]{:S(2)}) copy-start(f32[256,2,256]{0,2,1:T(8,128)} %get-tuple-element.83) | copy-start | bytes 1572868
  158.2 1.3 copy-start.12
  159.5 1.0 copy-start.5
  159.5 1.0 copy-start.14
  159.5 1.3 copy-start.16
  159.8 1.1 copy-start.3
  160.5 1.0 copy-start.18
  160.5 1.5 copy-start.11
  160.8 1.0 copy-start.7
  160.9 1.2 copy-start.9
  161.1 1.1 copy-start.2
  169.0 0.9 copy-start.13
  169.9 0.9 copy-start.15
  170.8 0.9 copy-start.17
  171.7 1.0 copy-start.4
  171.7 1.1 copy-start.19
  172.7 1.0 copy-start.8
  173.8 1.0 copy-start.10
  175.1 1.0 copy-start.20
  (8 other events, 5.7 us)
Sparse Core Ops, SparseCore 0:
  10.1 35.9 all-gather.1
where the time goes:
time: 188 us; the launch traced here: 187 us
  starting transfers between devices  67.4 us (36%)
  local copies, waits for them, and re-layouts  37.4 us (20%)
  matrix products  29.7 us (16%)
  waiting for transfers between devices  24.6 us (13%)
  between operations  14.7 us (8%)
  other arithmetic  13.1 us (7%)
    ppermute x6, starting transfers between devices, from_behind(): return lax.ppermute(value, axis, pairs)  33.5 us
    dot_general x14, matrix products, block_scores(): jnp.einsum('qhd,khd->qhk', expert_query, key_heads, preferred_element_typ...  22.5 us
    all_to_all x1, starting transfers between devices, body(): lax.all_to_all(outgoing, 'seq', split_axis=0, concat_axis=0, tiled=True)  22.4 us
    all_gather x1, waiting for transfers between devices, body(): piece = lax.all_gather(tokens, 'tp', axis=1, tiled=True)  18.3 us
    unnamed x98, local copies, waits for them, and re-layouts  13.9 us
    all_to_all x1, starting transfers between devices, body(): lax.all_to_all(labels, 'seq', split_axis=0, concat_axis=0, tiled=True)  11.4 us
    another operation x7, local copies, waits for them, and re-layouts, accumulate(): value_heads = block[:, 1].reshape(block_rows, local_heads, HD)  7.82 us
    ppermute x6, waiting for transfers between devices, from_behind(): return lax.ppermute(value, axis, pairs)  5.61 us
  transfers between devices with their start and end apart: 9, of which 2 were waited for; matrix products, arithmetic and copies ran while one was open for 32% of the time, Pallas kernels for 0%

commit v1 on v0

v1 whole, which is shorter than its diff:
```python
import functools
import math

import jax
import jax.numpy as jnp
from jax import lax
from jax.experimental import pallas as pl
from jax.sharding import PartitionSpec as P


HD = 128
TOPK = 2
PAGE = 16
BACK = 6


def from_behind(value, axis, by):
    peers = lax.axis_size(axis)
    pairs = [(i, i + by) for i in range(peers) if 0 <= i + by < peers]
    return lax.ppermute(value, axis, pairs)


def segment_info(positions, prompt_pages):
    ends = PAGE * jnp.cumsum(prompt_pages)
    below = ends[None, :] <= positions[:, None]
    segment = jnp.sum(below.astype(jnp.int32), axis=1)
    start = jnp.max(jnp.where(below, ends[None, :], 0), axis=1)
    return (segment, positions - start)


def rotate_heads(raw, offsets):
    half = HD // 2
    inverse = 10000.0 ** (-(2.0 * jnp.arange(half, dtype=jnp.float32)) / HD)
    angle = offsets.astype(jnp.float32)[:, None] * inverse[None, :]
    cosine = jnp.cos(angle)[:, None, :]
    sine = jnp.sin(angle)[:, None, :]
    lower = raw[..., :half]
    upper = raw[..., half:]
    return jnp.concatenate([lower * cosine - upper * sine, upper * cosine + lower * sine], axis=-1)


def attention_kernel(query_segment_ref, key_segment_ref, query_ref, *refs, blocks, scale):
    key_refs = refs[:blocks]
    value_refs = refs[blocks : 2 * blocks]
    out_ref = refs[2 * blocks]
    rows = query_ref.shape[0]
    query = query_ref[...]
    query_segment = query_segment_ref[...]
    row = lax.broadcasted_iota(jnp.int32, (rows, rows), 0)
    col = lax.broadcasted_iota(jnp.int32, (rows, rows), 1)

    def scores(distance):
        key = key_refs[distance][...]
        product = lax.dot_general(
            query, key, (((1,), (1,)), ((), ())), preferred_element_type=jnp.float32
        )
        allowed = query_segment == key_segment_ref[pl.ds(distance, 1), :]
        if distance == 0:
            allowed = allowed & (col <= row)
        return jnp.where(allowed, product * scale, -jnp.inf)

    peak = jnp.max(scores(0), axis=1, keepdims=True)
    for distance in range(1, blocks):
        peak = jnp.maximum(peak, jnp.max(scores(distance), axis=1, keepdims=True))
    total = jnp.zeros((rows, 1), jnp.float32)
    summed = jnp.zeros((rows, out_ref.shape[1]), jnp.float32)
    for distance in range(blocks):
        weight = jnp.exp(scores(distance) - peak)
        total = total + jnp.sum(weight, axis=1, keepdims=True)
        summed = summed + jnp.dot(
            weight.astype(jnp.bfloat16),
            value_refs[distance][...],
            preferred_element_type=jnp.float32,
        )
    out_ref[...] = (summed / total).astype(out_ref.dtype)


def attend(query, query_segment, key_segment, blocks_kv, local_heads):
    rows = query.shape[0]
    blocks = len(blocks_kv)
    grid = (local_heads, TOPK)
    query_spec = pl.BlockSpec((rows, HD), lambda h, e: (0, e * local_heads + h))
    key_spec = pl.BlockSpec((rows, HD), lambda h, e: (0, h))
    value_spec = pl.BlockSpec((rows, HD), lambda h, e: (0, local_heads + h))
    in_specs = (
        [
            pl.BlockSpec((rows, 1), lambda h, e: (0, 0)),
            pl.BlockSpec((blocks, rows), lambda h, e: (0, 0)),
            query_spec,
        ]
        + [key_spec] * blocks
        + [value_spec] * blocks
    )
    combos = local_heads * TOPK
    cost = pl.CostEstimate(
        flops=combos * 3 * blocks * 2 * rows * rows * HD,
        transcendentals=combos * blocks * rows * rows,
        bytes_accessed=2 * query.size * 2 + blocks * rows * 2 * local_heads * HD * 2,
    )
    kernel = functools.partial(attention_kernel, blocks=blocks, scale=1.0 / math.sqrt(HD))
    return pl.pallas_call(
        kernel,
        grid=grid,
        in_specs=in_specs,
        out_specs=query_spec,
        out_shape=jax.ShapeDtypeStruct(query.shape, jnp.bfloat16),
        cost_estimate=cost,
        name="block_attention",
    )(query_segment, key_segment, query, *blocks_kv, *blocks_kv)


def body(tokens, key_weight, value_weight, queries, prompt_pages, page_table):
    block_rows = tokens.shape[0]
    width = key_weight.shape[1]
    local_heads = width // HD
    devices = lax.axis_size("seq")
    first_row = lax.axis_index("seq") * block_rows
    positions = first_row + jnp.arange(block_rows, dtype=jnp.int32)
    segment, offsets = segment_info(positions, prompt_pages)
    piece = lax.all_gather(tokens, "tp", axis=1, tiled=True)
    raw_keys = jnp.dot(piece, key_weight, preferred_element_type=jnp.float32)
    raw_values = jnp.dot(piece, value_weight, preferred_element_type=jnp.float32)
    keys = rotate_heads(raw_keys.reshape(block_rows, local_heads, HD), offsets).astype(jnp.bfloat16)
    values = raw_values.astype(jnp.bfloat16)
    key_value = jnp.concatenate([keys.reshape(block_rows, width), values], axis=1)
    blocks = [key_value]
    for distance in range(1, BACK + 1):
        blocks.append(from_behind(key_value, "seq", distance))
    key_place = positions[None, :] - block_rows * jnp.arange(BACK + 1, dtype=jnp.int32)[:, None]
    key_segment, _ = segment_info(key_place.reshape(-1), prompt_pages)
    key_segment = jnp.where(key_place >= 0, key_segment.reshape(BACK + 1, block_rows), -1)
    query = queries.reshape(block_rows, TOPK * width)
    attended = attend(query, segment[:, None], key_segment, blocks, local_heads)
    attended = attended.reshape(block_rows, TOPK, width)
    pages_dev = block_rows // PAGE
    capacity = max(1, pages_dev // devices)
    owner = page_table // pages_dev
    place_on_owner = page_table % pages_dev
    page_order = jnp.arange(pages_dev, dtype=jnp.int32)
    earlier = (owner[:, None] == owner[None, :]) & (page_order[None, :] < page_order[:, None])
    rank = jnp.sum(earlier.astype(jnp.int32), axis=1)
    target = (owner[None, None, :] == jnp.arange(devices, dtype=jnp.int32)[:, None, None]) & (
        rank[None, None, :] == jnp.arange(capacity, dtype=jnp.int32)[None, :, None]
    )
    pages = key_value.reshape(pages_dev, PAGE, 2, width)
    page_index = jnp.sum(jnp.where(target, page_order[None, None, :], 0), axis=2)
    outgoing = pages[page_index.reshape(-1)]
    labels = jnp.sum(jnp.where(target, place_on_owner[None, None, :] + 1, 0), axis=2) - 1
    incoming = lax.all_to_all(outgoing, "seq", split_axis=0, concat_axis=0, tiled=True)
    arrived = lax.all_to_all(labels, "seq", split_axis=0, concat_axis=0, tiled=True)
    slots = jnp.arange(devices * capacity, dtype=jnp.int32)
    source_slot = jnp.sum(
        jnp.where(arrived.reshape(-1)[None, :] == page_order[:, None], slots[None, :], 0), axis=1
    )
    cache = incoming[source_slot]
    return (attended, cache)


def solution(mesh):
    in_specs = (P("seq", "tp"), P(None, "tp"), P(None, "tp"), P("seq", None, "tp"), P(), P("seq"))
    out_specs = (P("seq", None, "tp"), P("seq", None, None, "tp"))
    return jax.shard_map(body, mesh=mesh, in_specs=in_specs, out_specs=out_specs, check_vma=False)
```

time: 188 us -> 159 us (0.85)
  the two profiles are of different devices: /device:TPU:94 before, /device:TPU:6 now
where the time goes in v1:
time: 159 us
  waiting for transfers between devices  70.7 us (44%)
  starting transfers between devices  48.3 us (30%)
  between operations  14.4 us (9%)
  local copies, waits for them, and re-layouts  10.4 us (7%)
  other arithmetic  6.44 us (4%)
  Pallas kernels  6.25 us (4%)
  matrix products  2.19 us (1%)
    ppermute x6, waiting for transfers between devices, from_behind(): return lax.ppermute(value, axis, pairs)  44.9 us
    all_gather x1, waiting for transfers between devices, body(): piece = lax.all_gather(tokens, 'tp', axis=1, tiled=True)  25.2 us
    ppermute x6, starting transfers between devices, from_behind(): return lax.ppermute(value, axis, pairs)  24.9 us
    all_to_all x1, starting transfers between devices, body(): lax.all_to_all(labels, 'seq', split_axis=0, concat_axis=0, tiled=True)  12.8 us
    all_to_all x1, starting transfers between devices, body(): lax.all_to_all(outgoing, 'seq', split_axis=0, concat_axis=0, tiled=True)  10.6 us
    pallas_call x1, Pallas kernels, attend(): pl.pallas_call(kernel, grid=grid, in_specs=in_specs, out_specs=query_spec...  6.25 us
    unnamed x31, local copies, waits for them, and re-layouts  4.84 us
  transfers between devices with their start and end apart: 9, of which 5 were waited for; matrix products, arithmetic and copies ran while one was open for 10% of the time, Pallas kernels for 4%

profile of v1, /device:TPU:6, one launch (start us, length us, event | category | flops | bytes accessed | tf_op | source)
XLA Modules:
  0.0 158.6 jit_solution(6125256798090201876)
XLA Ops:
  7.2 0.0 copy-start
  7.2 0.0 all-gather.2.cloned.1.call-start
  7.2 0.7 all-gather.2.cloned.1.call-update
  8.0 0.2 convert_reduce_fusion.1
  8.1 0.1 select_reduce_fusion.1
  8.2 0.7 copy.47
  9.0 12.8 %all-to-all-start.1 = ((s32[64,1,1]{2,1,0:T(1,128)}), s32[64,1,1]{2,1,0:T(1,128)}, u32[]{:S(2)}, u32[]{:S(2)}) async-start(s32[64,1,1]{2,1,0:T(1,128)} %copy.47), calls=%async_computation.1 | async-start | bytes 65536 | tf_op jit(solution)/shard_map/all_to_all | solution.py:150
  21.8 0.0 copy-start.5
  21.8 0.6 copy-done.5
  22.4 0.1 copy.41
  22.6 0.1 multiply_reduce_fusion
  22.7 0.1 fusion.1
  22.8 1.2 multiply_cosine_fusion
  24.0 25.2 %all-gather.2.cloned.1.call-done = bf16[256,2048]{1,0:T(8,128)(2,1)} async-done(((bf16[256,256]{1,0:T(8,128)(2,1)}), bf16[256,2048]{1,0:T(8,128)(2,1)}) %all-gather.2.cloned.1.call-update) | async-done | bytes 1048592 | tf_op jit(solution)/shard_map/all_gather | solution.py:120
  49.2 1.7 %fusion.8 = f32[256,256]{0,1:T(8,128)S(1)} fusion(bf16[256,2048]{1,0:T(8,128)(2,1)} %all-gather.2.cloned.1.call-done, bf16[2048,256]{1,0:T(8,128)(2,1)S(1)} %copy-done), kind=kOutput, calls=%fused_computation.46 | convolution fusion | flops 268435456 | bytes 2359296 | tf_op jit(solution)/shard_map/dot_general | solution.py:121
  51.0 0.1 copy.50
  51.2 0.0 copy-start.2
  51.2 0.8 copy.51
  52.0 1.3 subtract_convert_fusion
  53.3 0.4 pad_maximum_fusion.1
  53.7 0.4 convolution_convert_fusion
  54.2 0.0 copy-start.3
  54.2 0.1 reshape.321
  54.3 1.6 gather_fusion
  55.9 10.6 %all-to-all-start = ((bf16[64,16,2,256]{3,1,2,0:T(8,128)(2,1)}), bf16[64,16,2,256]{3,1,2,0:T(8,128)(2,1)S(1)}, u32[]{:S(2)}, u32[]{:S(2)}) async-start(bf16[64,16,2,256]{3,1,2,0:T(8,128)(2,1)} %gather_fusion), calls=%async_computation | async-start | bytes 2097152 | tf_op jit(solution)/shard_map/all_to_all | solution.py:149
  66.5 0.1 broadcast_subtract_fusion
  66.6 0.1 convert_reduce_fusion
  66.7 0.8 copy.45.query_segment_ref
  67.5 0.7 copy.52
  68.2 3.4 %collective-permute-start = (bf16[256,512]{1,0:T(8,128)(2,1)S(1)}, bf16[256,512]{1,0:T(8,128)(2,1)S(1)}, u32[]{:S(2)}, u32[]{:S(2)}) collective-permute-start(bf16[256,512]{1,0:T(8,128)(2,1)S(1)} %pad_maximum_fusion.refs_0_.refs_7_), channel_id=1, source_target_pairs={{0,8},{8,16},{16,24},{24,32},{32,40},{40,48},{48,56},{56,64},{64,7... | collective-permute-start | bytes 786440 | tf_op jit(solution)/shard_map/ppermute | solution.py:20
  71.6 0.7 compare_select_fusion.1.key_segment_ref
  72.3 2.0 %reduce.3 = s32[64]{0:T(128)S(1)} reduce(s32[64,1,1]{2,1,0:T(1,128)} %all-to-all-done.1, s32[]{:T(128)} %constant.26.clone.1), dimensions={1,2}, to_apply=%all_to_all.8.reduce_sub_computation | reduce | bytes 516 | tf_op jit(solution)/shard_map/all_to_all | solution.py:150
  74.3 0.1 select_reduce_fusion
  74.4 4.3 %collective-permute-start.1 = (bf16[256,512]{1,0:T(8,128)(2,1)S(1)}, bf16[256,512]{1,0:T(8,128)(2,1)S(1)}, u32[]{:S(2)}, u32[]{:S(2)}) collective-permute-start(bf16[256,512]{1,0:T(8,128)(2,1)S(1)} %pad_maximum_fusion.refs_0_.refs_7_), channel_id=1, source_target_pairs={{0,16},{8,24},{16,32},{24,40},{32,48},{40,56},{48,64},{56,72},{64,... | collective-permute-start | bytes 786440 | tf_op jit(solution)/shard_map/ppermute | solution.py:20
  78.7 4.6 %collective-permute-start.2 = (bf16[256,512]{1,0:T(8,128)(2,1)S(1)}, bf16[256,512]{1,0:T(8,128)(2,1)S(1)}, u32[]{:S(2)}, u32[]{:S(2)}) collective-permute-start(bf16[256,512]{1,0:T(8,128)(2,1)S(1)} %pad_maximum_fusion.refs_0_.refs_7_), channel_id=1, source_target_pairs={{0,24},{8,32},{16,40},{24,48},{32,56},{40,64},{48,72},{56,80},{64,... | collective-permute-start | bytes 786440 | tf_op jit(solution)/shard_map/ppermute | solution.py:20
  83.3 5.2 %collective-permute-start.3 = (bf16[256,512]{1,0:T(8,128)(2,1)S(1)}, bf16[256,512]{1,0:T(8,128)(2,1)S(1)}, u32[]{:S(2)}, u32[]{:S(2)}) collective-permute-start(bf16[256,512]{1,0:T(8,128)(2,1)S(1)} %pad_maximum_fusion.refs_0_.refs_7_), channel_id=1, source_target_pairs={{0,32},{8,40},{16,48},{24,56},{32,64},{40,72},{48,80},{56,88},{64,... | collective-permute-start | bytes 786440 | tf_op jit(solution)/shard_map/ppermute | solution.py:20
  88.5 4.6 %collective-permute-start.4 = (bf16[256,512]{1,0:T(8,128)(2,1)S(1)}, bf16[256,512]{1,0:T(8,128)(2,1)S(1)}, u32[]{:S(2)}, u32[]{:S(2)}) collective-permute-start(bf16[256,512]{1,0:T(8,128)(2,1)S(1)} %pad_maximum_fusion.refs_0_.refs_7_), channel_id=1, source_target_pairs={{0,40},{8,48},{16,56},{24,64},{32,72},{40,80},{48,88},{56,96},{64,... | collective-permute-start | bytes 786440 | tf_op jit(solution)/shard_map/ppermute | solution.py:20
  93.1 7.3 %collective-permute-done.refs_1_.refs_8_ = bf16[256,512]{1,0:T(8,128)(2,1)S(1)} collective-permute-done((bf16[256,512]{1,0:T(8,128)(2,1)S(1)}, bf16[256,512]{1,0:T(8,128)(2,1)S(1)}, u32[]{:S(2)}, u32[]{:S(2)}) %collective-permute-start) | collective-permute-done | bytes 262176 | tf_op jit(solution)/shard_map/ppermute | solution.py:20
  100.5 2.8 %collective-permute-start.5 = (bf16[256,512]{1,0:T(8,128)(2,1)S(1)}, bf16[256,512]{1,0:T(8,128)(2,1)S(1)}, u32[]{:S(2)}, u32[]{:S(2)}) collective-permute-start(bf16[256,512]{1,0:T(8,128)(2,1)S(1)} %pad_maximum_fusion.refs_0_.refs_7_), channel_id=1, source_target_pairs={{0,48},{8,56},{16,64},{24,72},{32,80},{40,88},{48,96},{56,104},{64... | collective-permute-start | bytes 786440 | tf_op jit(solution)/shard_map/ppermute | solution.py:20
  103.3 10.3 %collective-permute-done.1.refs_2_.refs_9_ = bf16[256,512]{1,0:T(8,128)(2,1)S(1)} collective-permute-done((bf16[256,512]{1,0:T(8,128)(2,1)S(1)}, bf16[256,512]{1,0:T(8,128)(2,1)S(1)}, u32[]{:S(2)}, u32[]{:S(2)}) %collective-permute-start.1) | collective-permute-done | bytes 262176 | tf_op jit(solution)/shard_map/ppermute | solution.py:20
  113.7 13.2 %collective-permute-done.2.refs_3_.refs_10_ = bf16[256,512]{1,0:T(8,128)(2,1)S(1)} collective-permute-done((bf16[256,512]{1,0:T(8,128)(2,1)S(1)}, bf16[256,512]{1,0:T(8,128)(2,1)S(1)}, u32[]{:S(2)}, u32[]{:S(2)}) %collective-permute-start.2) | collective-permute-done | bytes 262176 | tf_op jit(solution)/shard_map/ppermute | solution.py:20
  126.9 14.0 %collective-permute-done.3.refs_4_.refs_11_ = bf16[256,512]{1,0:T(8,128)(2,1)S(1)} collective-permute-done((bf16[256,512]{1,0:T(8,128)(2,1)S(1)}, bf16[256,512]{1,0:T(8,128)(2,1)S(1)}, u32[]{:S(2)}, u32[]{:S(2)}) %collective-permute-start.3) | collective-permute-done | bytes 262176 | tf_op jit(solution)/shard_map/ppermute | solution.py:20
  140.8 0.8 copy-done.10
  141.6 0.7 copy-done.11
  142.3 6.2 %block_attention.1 = bf16[256,512]{1,0:T(8,128)(2,1)} custom-call(s32[256,1]{1,0:T(8,128)} %copy.45.query_segment_ref, s32[7,256]{1,0:T(8,128)} %compare_select_fusion.1.key_segment_ref, bf16[256,512]{1,0:T(8,128)(2,1)} %bitcast.27, bf16[256,512]{1,0:T(8,128)(2,1)} %copy-done.3, bf16[256,512]{1,0:T(8,128)(2,1)} %copy-done.6, bf16[256,512]{1,0:T(8,128)(2,1)} %copy-done.7, ...), custom_call_target="tpu_custom_call" | custom-call | flops 1409286144 | bytes 2359296 | tf_op jit(solution)/shard_map/block_attention/pallas_call | solution.py:101
  148.6 1.7 %reshape.320 = bf16[256,2,256]{2,1,0:T(2,128)(2,1)} reshape(bf16[256,512]{1,0:T(8,128)(2,1)} %block_attention.1) | data formatting | bytes 524288 | tf_op jit(solution)/shard_map/reshape | solution.py:134
  150.3 0.6 gather_fusion.1
  150.9 0.9 copy.48
  (41 shorter events, 0.3 us)
Async XLA Ops:
  7.2 42.0 %copy-start = (bf16[2048,256]{1,0:T(8,128)(2,1)S(1)}, bf16[2048,256]{1,0:T(8,128)(2,1)}, u32[]{:S(2)}) copy-start(bf16[2048,256]{1,0:T(8,128)(2,1)} %param.7) | copy-start | bytes 3145732
  7.2 0.7 copy-start.12
  7.2 42.0 %all-gather.2.cloned.1.call-start = ((), (), s32[]{:S(2)}) async-start(), calls=%async_computation.2 | async-start | bytes 1179648 | tf_op jit(solution)/shard_map/all_gather | solution.py:120
  9.0 47.0 %all-to-all-start.1 = ((s32[64,1,1]{2,1,0:T(1,128)}), s32[64,1,1]{2,1,0:T(1,128)}, u32[]{:S(2)}, u32[]{:S(2)}) async-start(s32[64,1,1]{2,1,0:T(1,128)} %copy.47), calls=%async_computation.1 | async-start | bytes 65536 | tf_op jit(solution)/shard_map/all_to_all | solution.py:150
  21.8 0.7 copy-start.5
  51.1 2.6 %copy-start.1 = (bf16[256,2048]{1,0:T(8,128)(2,1)S(1)}, bf16[256,2048]{1,0:T(8,128)(2,1)}, u32[]{:S(2)}) copy-start(bf16[256,2048]{1,0:T(8,128)(2,1)} %all-gather.2.cloned.1.call-done) | copy-start | bytes 3145732
  51.2 2.6 %copy-start.2 = (bf16[2048,256]{1,0:T(8,128)(2,1)S(1)}, bf16[2048,256]{1,0:T(8,128)(2,1)}, u32[]{:S(2)}) copy-start(bf16[2048,256]{1,0:T(8,128)(2,1)} %param.8) | copy-start | bytes 3145732
  54.2 46.3 %copy-start.3 = (bf16[256,512]{1,0:T(8,128)(2,1)}, bf16[256,512]{1,0:T(8,128)(2,1)S(1)}, u32[]{:S(2)}) copy-start(bf16[256,512]{1,0:T(8,128)(2,1)S(1)} %pad_maximum_fusion.refs_0_.refs_7_) | copy-start | bytes 786436
  55.9 11.6 %copy-start.4 = (bf16[256,2,256]{2,1,0:T(2,128)(2,1)S(1)}, bf16[256,2,256]{2,1,0:T(2,128)(2,1)}, u32[]{:S(2)}) copy-start(bf16[256,2,256]{2,1,0:T(2,128)(2,1)} %param.9) | copy-start | bytes 786436
  55.9 94.3 %all-to-all-start = ((bf16[64,16,2,256]{3,1,2,0:T(8,128)(2,1)}), bf16[64,16,2,256]{3,1,2,0:T(8,128)(2,1)S(1)}, u32[]{:S(2)}, u32[]{:S(2)}) async-start(bf16[64,16,2,256]{3,1,2,0:T(8,128)(2,1)} %gather_fusion), calls=%async_computation | async-start | bytes 2097152 | tf_op jit(solution)/shard_map/all_to_all | solution.py:149
  68.2 32.2 %collective-permute-start = (bf16[256,512]{1,0:T(8,128)(2,1)S(1)}, bf16[256,512]{1,0:T(8,128)(2,1)S(1)}, u32[]{:S(2)}, u32[]{:S(2)}) collective-permute-start(bf16[256,512]{1,0:T(8,128)(2,1)S(1)} %pad_maximum_fusion.refs_0_.refs_7_), channel_id=1, source_target_pairs={{0,8},{8,16},{16,24},{24,32},{32,40},{40,48},{48,56},{56,64},{64,7... | collective-permute-start | bytes 786440 | tf_op jit(solution)/shard_map/ppermute | solution.py:20
  74.4 39.3 %collective-permute-start.1 = (bf16[256,512]{1,0:T(8,128)(2,1)S(1)}, bf16[256,512]{1,0:T(8,128)(2,1)S(1)}, u32[]{:S(2)}, u32[]{:S(2)}) collective-permute-start(bf16[256,512]{1,0:T(8,128)(2,1)S(1)} %pad_maximum_fusion.refs_0_.refs_7_), channel_id=1, source_target_pairs={{0,16},{8,24},{16,32},{24,40},{32,48},{40,56},{48,64},{56,72},{64,... | collective-permute-start | bytes 786440 | tf_op jit(solution)/shard_map/ppermute | solution.py:20
  78.7 48.2 %collective-permute-start.2 = (bf16[256,512]{1,0:T(8,128)(2,1)S(1)}, bf16[256,512]{1,0:T(8,128)(2,1)S(1)}, u32[]{:S(2)}, u32[]{:S(2)}) collective-permute-start(bf16[256,512]{1,0:T(8,128)(2,1)S(1)} %pad_maximum_fusion.refs_0_.refs_7_), channel_id=1, source_target_pairs={{0,24},{8,32},{16,40},{24,48},{32,56},{40,64},{48,72},{56,80},{64,... | collective-permute-start | bytes 786440 | tf_op jit(solution)/shard_map/ppermute | solution.py:20
  83.3 57.5 %collective-permute-start.3 = (bf16[256,512]{1,0:T(8,128)(2,1)S(1)}, bf16[256,512]{1,0:T(8,128)(2,1)S(1)}, u32[]{:S(2)}, u32[]{:S(2)}) collective-permute-start(bf16[256,512]{1,0:T(8,128)(2,1)S(1)} %pad_maximum_fusion.refs_0_.refs_7_), channel_id=1, source_target_pairs={{0,32},{8,40},{16,48},{24,56},{32,64},{40,72},{48,80},{56,88},{64,... | collective-permute-start | bytes 786440 | tf_op jit(solution)/shard_map/ppermute | solution.py:20
  88.5 52.3 %collective-permute-start.4 = (bf16[256,512]{1,0:T(8,128)(2,1)S(1)}, bf16[256,512]{1,0:T(8,128)(2,1)S(1)}, u32[]{:S(2)}, u32[]{:S(2)}) collective-permute-start(bf16[256,512]{1,0:T(8,128)(2,1)S(1)} %pad_maximum_fusion.refs_0_.refs_7_), channel_id=1, source_target_pairs={{0,40},{8,48},{16,56},{24,64},{32,72},{40,80},{48,88},{56,96},{64,... | collective-permute-start | bytes 786440 | tf_op jit(solution)/shard_map/ppermute | solution.py:20
  100.5 41.8 %copy-start.6 = (bf16[256,512]{1,0:T(8,128)(2,1)}, bf16[256,512]{1,0:T(8,128)(2,1)S(1)}, u32[]{:S(2)}) copy-start(bf16[256,512]{1,0:T(8,128)(2,1)S(1)} %collective-permute-done.refs_1_.refs_8_) | copy-start | bytes 786436
  100.5 40.4 %collective-permute-start.5 = (bf16[256,512]{1,0:T(8,128)(2,1)S(1)}, bf16[256,512]{1,0:T(8,128)(2,1)S(1)}, u32[]{:S(2)}, u32[]{:S(2)}) collective-permute-start(bf16[256,512]{1,0:T(8,128)(2,1)S(1)} %pad_maximum_fusion.refs_0_.refs_7_), channel_id=1, source_target_pairs={{0,48},{8,56},{16,64},{24,72},{32,80},{40,88},{48,96},{56,104},{64... | collective-permute-start | bytes 786440 | tf_op jit(solution)/shard_map/ppermute | solution.py:20
  113.7 28.6 %copy-start.7 = (bf16[256,512]{1,0:T(8,128)(2,1)}, bf16[256,512]{1,0:T(8,128)(2,1)S(1)}, u32[]{:S(2)}) copy-start(bf16[256,512]{1,0:T(8,128)(2,1)S(1)} %collective-permute-done.1.refs_2_.refs_9_) | copy-start | bytes 786436
  126.9 15.4 %copy-start.8 = (bf16[256,512]{1,0:T(8,128)(2,1)}, bf16[256,512]{1,0:T(8,128)(2,1)S(1)}, u32[]{:S(2)}) copy-start(bf16[256,512]{1,0:T(8,128)(2,1)S(1)} %collective-permute-done.2.refs_3_.refs_10_) | copy-start | bytes 786436
  140.8 1.5 copy-start.9
  140.8 0.8 copy-start.10
  141.6 0.7 copy-start.11
Sparse Core Ops, SparseCore 0:
  10.1 39.0 all-gather.1
